TPU v7x, 32 devices: a whole 2x2x4 slice. The times are simulated.
32 devices in a mesh: row: 8 (over z, core), col: 4 (over y, x).
Axes of the slice: x: 2, y: 2, z: 4, core: 2. Of those that a mesh axis runs over, the one named last changes fastest.
Arguments:
- amplitudes: float32 [1024, 2048], P(('row', 'col')), may hold values from -6 to 6
- integral_tiles: float32 [1024, 128, 128], P(('row', 'col')), may hold values from -0.125 to 0.125
- tile_cd: int32 [1024], P(('row', 'col')), may hold values from 0 to 15, as said below
- tile_ab: int32 [1024], P(('row', 'col')), may hold values from 0 to 15
- tile_count: int32 [32], P(('row', 'col')), may hold values from 16 to 32, as said below
Outputs:
- residual: float32 [1024, 65536], P(None, ('row', 'col'))
Inputs may be any that keep to these rules, and one draw needn't show every extreme that they name: Every cd block carries one D2h irrep label of 8, the same for all sets, each label on 2 cd blocks; within a set every ab block carries a label likewise, each on 2 ab blocks; the 32 slots of a set hold exactly the (tile_cd, tile_ab) pairs whose labels are equal, each once, in an order that differs from set to set. `tile_count`: in every draw one set has all 32 slots live and another has 16.
All inputs are finite; a program needn't handle non-finite values.
Results may differ from a plain program's by a relative error of at most 0.0003.
Values sent between devices are 32-bit elements; how exact they have to be, the bound alone decides.
No kernel may reach another device: no remote copies, remote signals or barrier semaphores. Data moves between devices by JAX's collectives and lax.ppermute only.
A program may use at most 128 MiB of HBM per device.

v0:
```python
import jax
import jax.numpy as jnp
from jax import lax
from jax.sharding import PartitionSpec as P

BLK = 128
AB_DEV = 2048
CD = 2048
SLOTS = 32


def dense_block(group_tiles, set_cd, set_ab, nonempty_count):
    cd_blocks = CD // BLK
    ab_blocks = AB_DEV // BLK
    bucket_index = jnp.arange(SLOTS, dtype=jnp.int32)
    active_flags = (bucket_index < nonempty_count).astype(jnp.float32)
    packed_location = set_cd * ab_blocks + set_ab
    stacked_blocks = jnp.zeros((cd_blocks * ab_blocks, BLK, BLK), jnp.float32)
    stacked_blocks = stacked_blocks.at[packed_location].add(
        group_tiles * active_flags[:, None, None]
    )
    return (
        stacked_blocks.reshape(cd_blocks, ab_blocks, BLK, BLK)
        .transpose(0, 2, 1, 3)
        .reshape(CD, AB_DEV)
    )


def on_device(amplitudes, integral_tiles, tile_cd, tile_ab, tile_count):
    integrals = dense_block(integral_tiles, tile_cd, tile_ab, tile_count[0])
    return jnp.dot(
        lax.all_gather(amplitudes, ("row", "col"), axis=0, tiled=True),
        integrals,
        precision=lax.Precision.HIGHEST,
        preferred_element_type=jnp.float32,
    )


def solution(mesh):
    placed = (
        P(("row", "col"), None),
        P(("row", "col"), None, None),
        P(("row", "col")),
        P(("row", "col")),
        P(("row", "col")),
    )
    return jax.shard_map(
        on_device, mesh=mesh, in_specs=placed, out_specs=P(None, ("row", "col")), check_vma=False
    )
```

profile of v0, /device:TPU:0, one launch (start us, length us, event | category | flops | bytes accessed | tf_op | source)
XLA Modules:
  0.0 225.4 jit_solution(5875262002309532569)
XLA Ops:
  6.5 0.0 all-gather.2.cloned.1.call-start
  6.5 0.7 all-gather.2.cloned.1.call-update
  7.9 0.7 compare_select_fusion
  8.6 1.8 broadcast_multiply_fusion
  10.4 7.8 %broadcast_in_dim.7 = f32[256,128,128]{2,1,0:T(8,128)} broadcast(f32[]{:T(128)} %constant.0.clone.1), dimensions={} | broadcast | bytes 16777220 | tf_op jit(solution)/shard_map/broadcast_in_dim | solution.py:18
  18.2 6.4 %scatter_fusion = f32[256,128,128]{2,1,0:T(8,128)} fusion(f32[256,128,128]{2,1,0:T(8,128)} %broadcast_in_dim.7, s32[32]{0:T(128)S(1)} %compare_select_fusion, f32[32,128,128]{2,1,0:T(8,128)S(1)} %broadcast_multiply_fusion), kind=kCustom, calls=%fused_computation | custom fusion | flops 524288 | bytes 6291584 | tf_op jit(solution)/shard_map/scatter-add | solution.py:19
  24.6 17.7 %copy.7 = f32[16,16,128,128]{3,1,2,0:T(8,128)} copy(f32[16,16,128,128]{3,2,1,0:T(8,128)} %bitcast.14) | data formatting | bytes 33554432 | tf_op jit(solution)/shard_map/reshape | solution.py:23
  42.3 48.2 %all-gather.2.cloned.1.call-done = f32[1024,2048]{1,0:T(8,128)} async-done(((f32[32,2048]{1,0:T(8,128)}), f32[1024,2048]{1,0:T(8,128)}) %all-gather.2.cloned.1.call-update) | async-done | bytes 8388624 | tf_op jit(solution)/shard_map/all_gather | solution.py:32
  90.5 118.9 %fusion.3 = f32[1024,2048]{0,1:T(8,128)} fusion(f32[1024,2048]{1,0:T(8,128)} %all-gather.2.cloned.1.call-done, f32[256,8,16,128]{3,2,1,0:T(8,128)} %bitcast.15), kind=kOutput, calls=%fused_computation.4 | convolution fusion | flops 51539607552 | bytes 33554432 | tf_op jit(solution)/shard_map/dot_general | solution.py:31
  209.4 9.1 %copy.8 = f32[1024,2048]{1,0:T(8,128)} copy(f32[1024,2048]{0,1:T(8,128)} %fusion.3) | data formatting | bytes 16777216 | tf_op jit(solution)/shard_map/dot_general | solution.py:31
  (1 shorter events, 0.0 us)
Async XLA Ops:
  6.5 84.0 %all-gather.2.cloned.1.call-start = ((), (), s32[]{:S(2)}) async-start(), calls=%async_computation | async-start | bytes 8650752 | tf_op jit(solution)/shard_map/all_gather | solution.py:32
Sparse Core Ops, SparseCore 0:
  10.2 80.2 all-gather.1
where the time goes:
time: 226 us; the launch traced here: 225 us
  matrix products  119 us (53%)
  waiting for transfers between devices  48.9 us (22%)
  local copies, waits for them, and re-layouts  34.7 us (15%)
  between operations  14.1 us (6%)
  other arithmetic  8.88 us (4%)
    dot_general x1, matrix products, on_device(): jnp.dot(lax.all_gather(amplitudes, ('row', 'col'), axis=0, tiled=True), i...  119 us
    all_gather x1, waiting for transfers between devices, on_device(): lax.all_gather(amplitudes, ('row', 'col'), axis=0, tiled=True)  48.2 us
    reshape x1, local copies, waits for them, and re-layouts, dense_block(): stacked_blocks.reshape(cd_blocks, ab_blocks, BLK, BLK).transpose(0, 2, 1, 3)  17.7 us
    dot_general x1, local copies, waits for them, and re-layouts, on_device(): jnp.dot(lax.all_gather(amplitudes, ('row', 'col'), axis=0, tiled=True), i...  9.12 us
    broadcast_in_dim x1, local copies, waits for them, and re-layouts, dense_block(): stacked_blocks = jnp.zeros((cd_blocks * ab_blocks, BLK, BLK), jnp.float32)  7.84 us
    scatter-add x1, other arithmetic, dense_block(): stacked_blocks.at[packed_location]  6.41 us
  transfers between devices with their start and end apart: 1, of which 1 were waited for; matrix products, arithmetic and copies ran while one was open for 15% of the time, Pallas kernels for 0%

commit v1 on v0

v1 whole, which is shorter than its diff:
```python
import jax
import jax.numpy as jnp
from jax import lax
from jax.experimental import pallas as pl
from jax.experimental.pallas import tpu as pltpu
from jax.sharding import PartitionSpec as P

BLK = 128
AB_DEV = 2048
SLOTS = 32


def ladder_kernel(order_ref, cd_ref, live_ref, amp_ref, tile_ref, out_ref):
    k = pl.program_id(1)
    idx = pl.program_id(0) * pl.num_programs(1) + k

    @pl.when(k == 0)
    def _():
        out_ref[...] = jnp.zeros_like(out_ref)

    @pl.when(live_ref[idx] > 0)
    def _():
        out_ref[...] += jnp.dot(
            amp_ref[...],
            tile_ref[0],
            precision=lax.Precision.HIGHEST,
            preferred_element_type=jnp.float32,
        )


def sparse_ladder(amps, tiles, tile_cd, tile_ab, count):
    rows = amps.shape[0]
    ab_blocks = AB_DEV // BLK
    per_ab = SLOTS // ab_blocks
    order = jnp.argsort(tile_ab, stable=True).astype(jnp.int32)
    cd_sorted = tile_cd[order].astype(jnp.int32)
    live_sorted = (order < count).astype(jnp.int32)
    grid_spec = pltpu.PrefetchScalarGridSpec(
        num_scalar_prefetch=3,
        grid=(ab_blocks, per_ab),
        in_specs=[
            pl.BlockSpec((rows, BLK), lambda j, k, o, c, l: (0, c[j * per_ab + k])),
            pl.BlockSpec((1, BLK, BLK), lambda j, k, o, c, l: (o[j * per_ab + k], 0, 0)),
        ],
        out_specs=pl.BlockSpec((rows, BLK), lambda j, k, o, c, l: (0, j)),
    )
    return pl.pallas_call(
        ladder_kernel,
        grid_spec=grid_spec,
        out_shape=jax.ShapeDtypeStruct((rows, AB_DEV), jnp.float32),
        compiler_params=pltpu.CompilerParams(dimension_semantics=("arbitrary", "arbitrary")),
    )(order, cd_sorted, live_sorted, amps, tiles)


def on_device(amplitudes, integral_tiles, tile_cd, tile_ab, tile_count):
    amps = lax.all_gather(amplitudes, ("row", "col"), axis=0, tiled=True)
    return sparse_ladder(amps, integral_tiles, tile_cd, tile_ab, tile_count[0])


def solution(mesh):
    placed = (
        P(("row", "col"), None),
        P(("row", "col"), None, None),
        P(("row", "col")),
        P(("row", "col")),
        P(("row", "col")),
    )
    return jax.shard_map(
        on_device, mesh=mesh, in_specs=placed, out_specs=P(None, ("row", "col")), check_vma=False
    )
```

time: 226 us -> 128 us (0.57)
  matrix products: 119 us -> 0 us
  local copies, waits for them, and re-layouts: 34.7 us -> 1.23 us
  waiting for transfers between devices: 48.9 us -> 79.3 us
  Pallas kernels: 0 us -> 28.4 us
  other arithmetic: 8.88 us -> 2.79 us
    dot_general x1 -> x0, matrix products: 119 us -> none  [on_device(): jnp.dot(lax.all_gather(amplitudes, ('row', 'col'), axis=0, tiled=True), i...]
    all_gather x1, waiting for transfers between devices: 48.2 us -> 78.6 us  [on_device(): amps = lax.all_gather(amplitudes, ('row', 'col'), axis=0, tiled=True)]
    pallas_call x0 -> x1, Pallas kernels: none -> 28.4 us  [sparse_ladder(): pl.pallas_call(ladder_kernel, grid_spec=grid_spec, out_shape=jax.ShapeDty...]
    reshape x1 -> x0, local copies, waits for them, and re-layouts: 17.7 us -> none  [dense_block(): stacked_blocks.reshape(cd_blocks, ab_blocks, BLK, BLK).transpose(0, 2, 1, 3)]
    dot_general x1 -> x0, local copies, waits for them, and re-layouts: 9.12 us -> none  [on_device(): jnp.dot(lax.all_gather(amplitudes, ('row', 'col'), axis=0, tiled=True), i...]
    broadcast_in_dim x1 -> x0, local copies, waits for them, and re-layouts: 7.84 us -> none  [dense_block(): stacked_blocks = jnp.zeros((cd_blocks * ab_blocks, BLK, BLK), jnp.float32)]
    scatter-add x1 -> x0, other arithmetic: 6.41 us -> none  [dense_block(): stacked_blocks.at[packed_location]]
  transfers between devices with their start and end apart: 1 -> 1, of which waited for: 1 -> 1; matrix products, arithmetic and copies ran while one was open for 15% -> 3% of each run, Pallas kernels for 0% -> 0%
where the time goes in v1:
time: 128 us; the launch traced here: 126 us
  waiting for transfers between devices  79.3 us (62%)
  Pallas kernels  28.4 us (22%)
  between operations  14.1 us (11%)
  other arithmetic  2.79 us (2%)
    all_gather x1, waiting for transfers between devices, on_device(): amps = lax.all_gather(amplitudes, ('row', 'col'), axis=0, tiled=True)  78.6 us
    pallas_call x1, Pallas kernels, sparse_ladder(): pl.pallas_call(ladder_kernel, grid_spec=grid_spec, out_shape=jax.ShapeDty...  28.4 us
  transfers between devices with their start and end apart: 1, of which 1 were waited for; matrix products, arithmetic and copies ran while one was open for 3% of the time, Pallas kernels for 0%

profile of v1, /device:TPU:0, one launch (start us, length us, event | category | flops | bytes accessed | tf_op | source)
XLA Modules:
  0.0 125.8 jit_solution(13690745916448690877)
XLA Ops:
  6.5 0.0 copy-start
  6.5 0.0 all-gather.2.cloned.1.call-start
  6.5 0.7 all-gather.2.cloned.1.call-update
  7.9 2.3 %sort.17 = (s32[32]{0:T(128)}, s32[32]{0:T(128)S(1)}) sort(s32[32]{0:T(128)} %param.8, s32[32]{0:T(128)S(1)} %iota.4), dimensions={0}, to_apply=%region_0.0 | sort | flops 160 | bytes 512 | tf_op jit(solution)/shard_map/jit(argsort)/sort | solution.py:35
  10.2 0.0 copy-start.1
  10.2 0.0 copy-done
  10.2 1.2 gather_fusion
  11.4 0.5 compare_convert_fusion.live_ref
  11.9 78.6 %all-gather.2.cloned.1.call-done.amp_ref = f32[1024,2048]{1,0:T(8,128)} async-done(((f32[32,2048]{1,0:T(8,128)}), f32[1024,2048]{1,0:T(8,128)}) %all-gather.2.cloned.1.call-update) | async-done | bytes 8388624 | tf_op jit(solution)/shard_map/all_gather | solution.py:56
  90.5 0.0 copy-done.1
  90.5 28.4 %shard_map.55 = f32[1024,2048]{1,0:T(8,128)} custom-call(s32[32]{0:T(128)} %copy-done.1, s32[32]{0:T(128)} %gather_fusion, s32[32]{0:T(128)} %compare_convert_fusion.live_ref, f32[1024,2048]{1,0:T(8,128)} %all-gather.2.cloned.1.call-done.amp_ref, f32[32,128,128]{2,1,0:T(8,128)} %tile_ref.1), custom_call_target="tpu_custom_call" | custom-call | tf_op jit(solution)/shard_map/pallas_call | solution.py:47
  (3 shorter events, 0.0 us)
Async XLA Ops:
  6.5 3.7 %copy-start = (s32[32]{0:T(128)S(1)}, s32[32]{0:T(128)}, u32[]{:S(2)}) copy-start(s32[32]{0:T(128)} %param.7) | copy-start | bytes 388
  6.5 84.0 %all-gather.2.cloned.1.call-start = ((), (), s32[]{:S(2)}) async-start(), calls=%async_computation | async-start | bytes 8650752 | tf_op jit(solution)/shard_map/all_gather | solution.py:56
  10.2 80.3 %copy-start.1 = (s32[32]{0:T(128)}, s32[32]{0:T(128)S(1)}, u32[]{:S(2)}) copy-start(s32[32]{0:T(128)S(1)} %get-tuple-element.6.order_ref) | copy-start | bytes 388
Sparse Core Ops, SparseCore 0:
  10.2 80.2 all-gather.1

commit v2 on v1

v2 whole, which is shorter than its diff:
```python
import jax
import jax.numpy as jnp
from jax import lax
from jax.experimental import pallas as pl
from jax.experimental.pallas import tpu as pltpu
from jax.sharding import PartitionSpec as P

BLK = 128
AB_DEV = 2048
SLOTS = 32
ROW_TILE = 256


def split_dot(a, b):
    a_hi = a.astype(jnp.bfloat16)
    a_lo = (a - a_hi.astype(jnp.float32)).astype(jnp.bfloat16)
    b_hi = b.astype(jnp.bfloat16)
    b_lo = (b - b_hi.astype(jnp.float32)).astype(jnp.bfloat16)

    def dot(x, y):
        return jnp.dot(x, y, preferred_element_type=jnp.float32)

    return dot(a_hi, b_hi) + (dot(a_hi, b_lo) + dot(a_lo, b_hi))


def make_kernel(ab_blocks, per_ab):
    def ladder_kernel(order_ref, cd_ref, live_ref, amp_ref, tile_ref, out_ref):
        for j in range(ab_blocks):
            acc = None
            for k in range(per_ab):
                idx = j * per_ab + k
                part = split_dot(amp_ref[cd_ref[idx]], tile_ref[order_ref[idx]])
                part = jnp.where(live_ref[idx] > 0, part, 0.0)
                acc = part if acc is None else acc + part
            out_ref[:, j * BLK:(j + 1) * BLK] = acc

    return ladder_kernel


def slot_tables(tile_cd, tile_ab, count):
    n = tile_ab.shape[0]
    slot = jnp.arange(n, dtype=jnp.int32)
    key = tile_ab.astype(jnp.int32) * n + slot
    rank = jnp.sum((key[None, :] < key[:, None]).astype(jnp.int32), axis=1)
    hit = rank[None, :] == slot[:, None]
    order = jnp.sum(jnp.where(hit, slot[None, :], 0), axis=1)
    cd_sorted = jnp.sum(jnp.where(hit, tile_cd[None, :].astype(jnp.int32), 0), axis=1)
    live_sorted = (order < count).astype(jnp.int32)
    return order, cd_sorted, live_sorted


def sparse_ladder(amp3, tiles, tile_cd, tile_ab, count):
    ncd, rows, _ = amp3.shape
    ab_blocks = AB_DEV // BLK
    per_ab = SLOTS // ab_blocks
    order, cd_sorted, live_sorted = slot_tables(tile_cd, tile_ab, count)
    grid_spec = pltpu.PrefetchScalarGridSpec(
        num_scalar_prefetch=3,
        grid=(rows // ROW_TILE,),
        in_specs=[
            pl.BlockSpec((ncd, ROW_TILE, BLK), lambda i, o, c, l: (0, i, 0)),
            pl.BlockSpec(tiles.shape, lambda i, o, c, l: (0, 0, 0)),
        ],
        out_specs=pl.BlockSpec((ROW_TILE, AB_DEV), lambda i, o, c, l: (i, 0)),
    )
    return pl.pallas_call(
        make_kernel(ab_blocks, per_ab),
        grid_spec=grid_spec,
        out_shape=jax.ShapeDtypeStruct((rows, AB_DEV), jnp.float32),
    )(order, cd_sorted, live_sorted, amp3, tiles)


def on_device(amplitudes, integral_tiles, tile_cd, tile_ab, tile_count):
    rows, cd = amplitudes.shape
    local = amplitudes.reshape(rows, cd // BLK, BLK).transpose(1, 0, 2)
    amp3 = lax.all_gather(local, ("row", "col"), axis=1, tiled=True)
    return sparse_ladder(amp3, integral_tiles, tile_cd, tile_ab, tile_count[0])


def solution(mesh):
    placed = (
        P(("row", "col"), None),
        P(("row", "col"), None, None),
        P(("row", "col")),
        P(("row", "col")),
        P(("row", "col")),
    )
    return jax.shard_map(
        on_device, mesh=mesh, in_specs=placed, out_specs=P(None, ("row", "col")), check_vma=False
    )
```

time: 128 us -> 110 us (0.86); the launches traced: 126 us -> 110 us
  Pallas kernels: 28.4 us -> 12.2 us
    pallas_call x1, Pallas kernels: 28.4 us -> 12.2 us  [sparse_ladder(): pl.pallas_call(make_kernel(ab_blocks, per_ab), grid_spec=grid_spec, out_s...]
    sort x1 -> x0, other arithmetic: 2.26 us -> none  [sparse_ladder(): order = jnp.argsort(tile_ab, stable=True).astype(jnp.int32)]
    reduce_sum x0 -> x2, other arithmetic: none -> 1.44 us  [the longest x1 1.26 us: slot_tables(): jnp.sum(jnp.where(hit, tile_cd[None, :].astype(jnp.int32), 0), axis=1)]
  transfers between devices with their start and end apart: 1 -> 1, of which waited for: 1 -> 1; matrix products, arithmetic and copies ran while one was open for 3% -> 2% of each run, Pallas kernels for 0% -> 0%
where the time goes in v2:
time: 110 us
  waiting for transfers between devices  79.2 us (72%)
  between operations  14 us (13%)
  Pallas kernels  12.2 us (11%)
  other arithmetic  2.62 us (2%)
  local copies, waits for them, and re-layouts  1.68 us (2%)
    all_gather x1, waiting for transfers between devices, on_device(): amp3 = lax.all_gather(local, ('row', 'col'), axis=1, tiled=True)  79.2 us
    pallas_call x1, Pallas kernels, sparse_ladder(): pl.pallas_call(make_kernel(ab_blocks, per_ab), grid_spec=grid_spec, out_s...  12.2 us
  transfers between devices with their start and end apart: 1, of which 1 were waited for; matrix products, arithmetic and copies ran while one was open for 2% of the time, Pallas kernels for 0%

profile of v2, /device:TPU:0, one launch (start us, length us, event | category | flops | bytes accessed | tf_op | source)
XLA Modules:
  0.0 109.7 jit_solution(4945810497462101903)
XLA Ops:
  6.5 0.0 copy-start
  6.5 0.0 all-gather.2.cloned.1.call-start
  6.5 0.9 copy-done
  7.5 0.7 bitcast_bitcast_fusion
  8.2 0.0 all-gather.2.cloned.1.call-update
  8.9 0.7 iota_add_fusion
  9.5 0.2 convert_reduce_fusion
  9.7 1.3 %select_reduce_fusion = (s32[32]{0:T(128)}, s32[32]{0:T(128)S(1)}) fusion(s32[32]{0:T(128)} %param.7, s32[32]{0:T(128)S(1)} %convert_reduce_fusion), kind=kLoop, calls=%fused_computation.1 | loop fusion | flops 5056 | bytes 512 | tf_op jit(solution)/shard_map/reduce_sum | solution.py:47
  11.0 0.0 copy-start.1
  11.0 0.5 compare_convert_fusion.live_ref
  11.5 79.2 %all-gather.2.cloned.1.call-done.amp_ref = f32[16,1024,128]{2,1,0:T(8,128)} async-done(((f32[16,32,128]{2,1,0:T(8,128)}), f32[16,1024,128]{2,1,0:T(8,128)}) %all-gather.2.cloned.1.call-update) | async-done | bytes 8388624 | tf_op jit(solution)/shard_map/all_gather | solution.py:76
  90.7 0.0 copy-done.1
  90.7 12.2 %shard_map.55 = f32[1024,2048]{1,0:T(8,128)} custom-call(s32[32]{0:T(128)} %copy-done.1, s32[32]{0:T(128)} %get-tuple-element.5.cd_ref, s32[32]{0:T(128)} %compare_convert_fusion.live_ref, f32[16,1024,128]{2,1,0:T(8,128)} %all-gather.2.cloned.1.call-done.amp_ref, f32[32,128,128]{2,1,0:T(8,128)} %tile_ref.1), custom_call_target="tpu_custom_call" | custom-call | tf_op jit(solution)/shard_map/pallas_call | solution.py:66
Async XLA Ops:
  6.5 1.0 copy-start
  6.5 84.2 %all-gather.2.cloned.1.call-start = ((), (), s32[]{:S(2)}) async-start(), calls=%async_computation | async-start | bytes 8650752 | tf_op jit(solution)/shard_map/all_gather | solution.py:76
  11.0 79.7 %copy-start.1 = (s32[32]{0:T(128)}, s32[32]{0:T(128)S(1)}, u32[]{:S(2)}) copy-start(s32[32]{0:T(128)S(1)} %get-tuple-element.6.order_ref) | copy-start | bytes 388
Sparse Core Ops, SparseCore 0:
  10.3 80.3 all-gather.1

commit v3 on v2

--- a/solution.py
+++ b/solution.py
@@ -11,25 +11,34 @@
 ROW_TILE = 256
 
 
-def split_dot(a, b):
-    a_hi = a.astype(jnp.bfloat16)
-    a_lo = (a - a_hi.astype(jnp.float32)).astype(jnp.bfloat16)
-    b_hi = b.astype(jnp.bfloat16)
-    b_lo = (b - b_hi.astype(jnp.float32)).astype(jnp.bfloat16)
+def split_f32(x):
+    hi = x.astype(jnp.bfloat16)
+    return hi, (x - hi.astype(jnp.float32)).astype(jnp.bfloat16)
 
+
+def split_tiles(x):
+    hi = lax.reduce_precision(x, exponent_bits=8, mantissa_bits=7)
+    return hi.astype(jnp.bfloat16), (x - hi).astype(jnp.bfloat16)
+
+
+def make_kernel(ncd, ab_blocks, per_ab):
     def dot(x, y):
         return jnp.dot(x, y, preferred_element_type=jnp.float32)
 
-    return dot(a_hi, b_hi) + (dot(a_hi, b_lo) + dot(a_lo, b_hi))
-
-
-def make_kernel(ab_blocks, per_ab):
-    def ladder_kernel(order_ref, cd_ref, live_ref, amp_ref, tile_ref, out_ref):
+    def ladder_kernel(order_ref, cd_ref, live_ref, amp_ref, hi_ref, lo_ref, out_ref, ahi_ref, alo_ref):
+        for c in range(ncd):
+            a_hi, a_lo = split_f32(amp_ref[c])
+            ahi_ref[c] = a_hi
+            alo_ref[c] = a_lo
         for j in range(ab_blocks):
             acc = None
             for k in range(per_ab):
                 idx = j * per_ab + k
-                part = split_dot(amp_ref[cd_ref[idx]], tile_ref[order_ref[idx]])
+                c = cd_ref[idx]
+                s = order_ref[idx]
+                a_hi = ahi_ref[c]
+                t_hi = hi_ref[s]
+                part = dot(a_hi, t_hi) + (dot(a_hi, lo_ref[s]) + dot(alo_ref[c], t_hi))
                 part = jnp.where(live_ref[idx] > 0, part, 0.0)
                 acc = part if acc is None else acc + part
             out_ref[:, j * BLK:(j + 1) * BLK] = acc
@@ -54,20 +63,26 @@
     ab_blocks = AB_DEV // BLK
     per_ab = SLOTS // ab_blocks
     order, cd_sorted, live_sorted = slot_tables(tile_cd, tile_ab, count)
+    t_hi, t_lo = split_tiles(tiles)
     grid_spec = pltpu.PrefetchScalarGridSpec(
         num_scalar_prefetch=3,
         grid=(rows // ROW_TILE,),
         in_specs=[
             pl.BlockSpec((ncd, ROW_TILE, BLK), lambda i, o, c, l: (0, i, 0)),
-            pl.BlockSpec(tiles.shape, lambda i, o, c, l: (0, 0, 0)),
+            pl.BlockSpec(t_hi.shape, lambda i, o, c, l: (0, 0, 0)),
+            pl.BlockSpec(t_lo.shape, lambda i, o, c, l: (0, 0, 0)),
         ],
         out_specs=pl.BlockSpec((ROW_TILE, AB_DEV), lambda i, o, c, l: (i, 0)),
+        scratch_shapes=[
+            pltpu.VMEM((ncd, ROW_TILE, BLK), jnp.bfloat16),
+            pltpu.VMEM((ncd, ROW_TILE, BLK), jnp.bfloat16),
+        ],
     )
     return pl.pallas_call(
-        make_kernel(ab_blocks, per_ab),
+        make_kernel(ncd, ab_blocks, per_ab),
         grid_spec=grid_spec,
         out_shape=jax.ShapeDtypeStruct((rows, AB_DEV), jnp.float32),
-    )(order, cd_sorted, live_sorted, amp3, tiles)
+    )(order, cd_sorted, live_sorted, amp3, t_hi, t_lo)
 
 
 def on_device(amplitudes, integral_tiles, tile_cd, tile_ab, tile_count):

time: 110 us -> 111 us (level)
  other arithmetic: 2.62 us -> 6.34 us
  waiting for transfers between devices: 79.2 us -> 75.5 us
    all_gather x1, waiting for transfers between devices: 79.2 us -> 75.5 us  [on_device(): amp3 = lax.all_gather(local, ('row', 'col'), axis=1, tiled=True)]
    convert_element_type x0 -> x1, other arithmetic: none -> 3.58 us  [split_tiles(): return (hi.astype(jnp.bfloat16), (x - hi).astype(jnp.bfloat16))]
  transfers between devices with their start and end apart: 1 -> 1, of which waited for: 1 -> 1; matrix products, arithmetic and copies ran while one was open for 2% -> 6% of each run, Pallas kernels for 0% -> 0%
where the time goes in v3:
time: 111 us; the launch traced here: 110 us
  waiting for transfers between devices  75.5 us (68%)
  between operations  14 us (13%)
  Pallas kernels  12.7 us (11%)
  other arithmetic  6.34 us (6%)
  local copies, waits for them, and re-layouts  1.68 us (2%)
    all_gather x1, waiting for transfers between devices, on_device(): amp3 = lax.all_gather(local, ('row', 'col'), axis=1, tiled=True)  75.5 us
    pallas_call x1, Pallas kernels, sparse_ladder(): pl.pallas_call(make_kernel(ncd, ab_blocks, per_ab), grid_spec=grid_spec,...  12.7 us
    convert_element_type x1, other arithmetic, split_tiles(): return (hi.astype(jnp.bfloat16), (x - hi).astype(jnp.bfloat16))  3.58 us
  transfers between devices with their start and end apart: 1, of which 1 were waited for; matrix products, arithmetic and copies ran while one was open for 6% of the time, Pallas kernels for 0%

profile of v3, /device:TPU:0, one launch (start us, length us, event | category | flops | bytes accessed | tf_op | source)
XLA Modules:
  0.0 110.3 jit_solution(9543122964844734245)
XLA Ops:
  6.5 0.0 copy-start
  6.5 0.0 all-gather.2.cloned.1.call-start
  6.5 0.9 copy-done
  7.5 0.7 bitcast_bitcast_fusion
  8.2 0.0 all-gather.2.cloned.1.call-update
  8.9 0.7 iota_add_fusion
  9.5 0.2 convert_reduce_fusion
  9.7 1.3 %select_reduce_fusion = (s32[32]{0:T(128)}, s32[32]{0:T(128)S(1)}) fusion(s32[32]{0:T(128)} %param.7, s32[32]{0:T(128)S(1)} %convert_reduce_fusion), kind=kLoop, calls=%fused_computation.4 | loop fusion | flops 5056 | bytes 512 | tf_op jit(solution)/shard_map/reduce_sum | solution.py:56
  11.1 0.0 copy-start.1
  11.1 0.6 compare_convert_fusion.live_ref
  11.7 3.6 %fusion = (bf16[32,128,128]{2,1,0:T(8,128)(2,1)}, bf16[32,128,128]{2,1,0:T(8,128)(2,1)}) fusion(f32[32,128,128]{2,1,0:T(8,128)} %param.6), kind=kLoop, calls=%fused_computation.2 | loop fusion | flops 2097152 | bytes 4194304 | tf_op jit(solution)/shard_map/convert_element_type | solution.py:21
  15.2 0.0 copy-done.1
  15.2 75.5 %all-gather.2.cloned.1.call-done.amp_ref = f32[16,1024,128]{2,1,0:T(8,128)} async-done(((f32[16,32,128]{2,1,0:T(8,128)}), f32[16,1024,128]{2,1,0:T(8,128)}) %all-gather.2.cloned.1.call-update) | async-done | bytes 8388624 | tf_op jit(solution)/shard_map/all_gather | solution.py:91
  90.7 12.7 %shard_map.55 = f32[1024,2048]{1,0:T(8,128)} custom-call(s32[32]{0:T(128)} %copy-done.1, s32[32]{0:T(128)} %get-tuple-element.5.cd_ref, s32[32]{0:T(128)} %compare_convert_fusion.live_ref, f32[16,1024,128]{2,1,0:T(8,128)} %all-gather.2.cloned.1.call-done.amp_ref, bf16[32,128,128]{2,1,0:T(8,128)(2,1)} %get-tuple-element.8.hi_ref, ...), custom_call_target="tpu_custom_call" | custom-call | tf_op jit(solution)/shard_map/pallas_call | solution.py:81
Async XLA Ops:
  6.5 1.0 copy-start
  6.5 84.2 %all-gather.2.cloned.1.call-start = ((), (), s32[]{:S(2)}) async-start(), calls=%async_computation | async-start | bytes 8650752 | tf_op jit(solution)/shard_map/all_gather | solution.py:91
  11.1 4.2 %copy-start.1 = (s32[32]{0:T(128)}, s32[32]{0:T(128)S(1)}, u32[]{:S(2)}) copy-start(s32[32]{0:T(128)S(1)} %get-tuple-element.6.order_ref) | copy-start | bytes 388
Sparse Core Ops, SparseCore 0:
  10.3 80.3 all-gather.1
